TPU v7x, 512 devices: a whole 4x4x16 slice. The times are simulated.
512 devices in a mesh: dp: 64 (over z, x_lo, core), tensor: 8 (over y, x_hi).
Axes of the slice: x: 4 (x_hi: 2, x_lo: 2; x = x_hi * 2 + x_lo), y: 4, z: 16, core: 2. Of those that a mesh axis runs over, the one named last changes fastest.
Arguments:
- hidden_in: bfloat16 [16384, 4096], P(('dp', 'tensor')), may hold values from -12 to 12
- norm_gain: bfloat16 [4096], replicated, may hold values from 0.5 to 1.5
- w_query: bfloat16 [4096, 4096], P('dp', 'tensor'), may hold values from -0.11328125 to 0.11328125
- w_key: bfloat16 [4096, 1024], P('dp', 'tensor'), may hold values from -0.11328125 to 0.11328125
- w_value: bfloat16 [4096, 1024], P('dp', 'tensor'), may hold values from -0.09375 to 0.09375
- w_out: bfloat16 [4096, 4096], P('tensor', 'dp'), may hold values from -0.09375 to 0.09375
- segment: int32 [16384], P('dp'), may hold values from -1 to 1, as said below
Outputs:
- hidden_out: bfloat16 [16384, 4096], P(('dp', 'tensor'))
- kv_cache: bfloat16 [16384, 8, 256], P('dp', 'tensor')
Inputs may be any that keep to these rules, and one draw needn't show every extreme that they name: `segment`: within each pack of 256 rows, prompts are numbered from 0 in order and each starts at a multiple of 128; a prompt's last tile may end in rows of -1, and whole tiles of -1 may only follow the last prompt of a pack; the first tile of every pack holds a prompt; in every draw some pack has no tile of -1 only and holds one prompt a tile.
All inputs are finite; a program needn't handle non-finite values.
Results may differ from a plain program's by a relative error of at most 0.0085.
Values may be sent and summed in bfloat16 or wider, within the bound.
No kernel may reach another device: no remote copies, remote signals or barrier semaphores. Data moves between devices by JAX's collectives and lax.ppermute only.
A program may use at most 64 MiB of HBM per device.

v0:
```python
import jax
import jax.numpy as jnp
from jax import lax
from jax.sharding import PartitionSpec as P

HEAD = 128
rope_theta = 500000.0
norm_epsilon = 1e-05


def inverse_frequency(head_width):
    exponent = jnp.arange(0, head_width, 2).astype(jnp.float32) / head_width
    base_freq = rope_theta ** (-exponent)
    wavelength = 2.0 * jnp.pi / base_freq
    smooth = (8192.0 / wavelength - 1.0) / 3.0
    blended = (1.0 - smooth) * base_freq / 8.0 + smooth * base_freq
    return jnp.where(
        wavelength < 2048.0, base_freq, jnp.where(wavelength > 8192.0, base_freq / 8.0, blended)
    )


def positions_of(segment):
    row_index = jnp.arange(segment.shape[0], dtype=jnp.int32)
    changed = jnp.concatenate([jnp.ones((1,), dtype=bool), segment[1:] != segment[:-1]])
    begins = lax.cummax(jnp.where(changed, row_index, 0), axis=0)
    return row_index - begins


def rotate(vectors, position):
    head_width = vectors.shape[-1]
    half_width = head_width // 2
    angles = position.astype(jnp.float32)[:, None] * inverse_frequency(head_width)[None, :]
    cosine = jnp.concatenate([jnp.cos(angles), jnp.cos(angles)], axis=-1)[:, None, :]
    sine_table = jnp.concatenate([jnp.sin(angles), jnp.sin(angles)], axis=-1)[:, None, :]
    turned = jnp.concatenate([-vectors[..., half_width:], vectors[..., :half_width]], axis=-1)
    return vectors * cosine + turned * sine_table


def rms_normed(rows_float, norm_gain):
    mean_square = jnp.mean(rows_float * rows_float, axis=-1, keepdims=True)
    return (
        rows_float * lax.rsqrt(mean_square + norm_epsilon) * norm_gain.astype(jnp.float32)
    ).astype(jnp.bfloat16)


def visible_pairs(segment, key_count):
    row_index = jnp.arange(segment.shape[0], dtype=jnp.int32)
    key_index = jnp.arange(key_count, dtype=jnp.int32)
    same_segment = (segment[:, None] == segment[None, :]) & (segment[:, None] >= 0)
    causal = key_index[None, :] <= row_index[:, None]
    return same_segment & causal | (key_index[None, :] == row_index[:, None])


def body(hidden_in, norm_gain, w_query, w_key, w_value, w_out, segment):
    pack_rows = segment.shape[0]
    query_cols = w_query.shape[1]
    kv_cols = w_key.shape[1]
    query_heads = query_cols // HEAD
    kv_heads = kv_cols // HEAD
    group_size = query_heads // kv_heads
    score_scale = HEAD ** (-0.5)
    rows_float = hidden_in.astype(jnp.float32)
    normed = rms_normed(rows_float, norm_gain)
    gathered = lax.all_gather(normed, "tensor", axis=0, tiled=True)
    joined = jnp.concatenate(
        (
            lax.all_gather(w_query, "dp", axis=0, tiled=True),
            lax.all_gather(w_key, "dp", axis=0, tiled=True),
            lax.all_gather(w_value, "dp", axis=0, tiled=True),
        ),
        axis=1,
    )
    projected = jnp.dot(gathered, joined, preferred_element_type=jnp.float32)
    position = positions_of(segment)
    query_rows = rotate(
        projected[:, :query_cols].reshape(pack_rows, query_heads, HEAD), position
    ).astype(jnp.bfloat16)
    key_rows = rotate(
        projected[:, query_cols : query_cols + kv_cols].reshape(pack_rows, kv_heads, HEAD), position
    ).astype(jnp.bfloat16)
    value_rows = (
        projected[:, query_cols + kv_cols :].astype(jnp.bfloat16).reshape(pack_rows, kv_heads, HEAD)
    )
    cache_rows = jnp.concatenate([key_rows, value_rows], axis=-1)
    grouped_query = query_rows.reshape(pack_rows, kv_heads, group_size, HEAD)
    scores = (
        jnp.einsum("skgh,tkh->kgst", grouped_query, key_rows, preferred_element_type=jnp.float32)
        * score_scale
    )
    allowed = visible_pairs(segment, pack_rows)
    scores = jnp.where(allowed, scores, -1e30)
    row_max = jnp.max(scores, axis=-1, keepdims=True)
    weight = jnp.exp(scores - row_max)
    weight_sum = jnp.sum(weight, axis=-1)
    mixed_rows = (
        jnp.einsum(
            "kgst,tkh->kgsh",
            weight.astype(jnp.bfloat16),
            value_rows,
            preferred_element_type=jnp.float32,
        )
        / weight_sum[..., None]
    )
    attended = (
        jnp.transpose(mixed_rows, (2, 0, 1, 3)).astype(jnp.bfloat16).reshape(pack_rows, query_cols)
    )
    out_full = lax.all_gather(w_out, "dp", axis=1, tiled=True)
    summed = lax.psum_scatter(
        jnp.dot(attended, out_full, preferred_element_type=jnp.float32).astype(jnp.bfloat16),
        "tensor",
        scatter_dimension=0,
        tiled=True,
    ).astype(jnp.float32)
    hidden_out = (summed + rows_float).astype(jnp.bfloat16)
    return (hidden_out, cache_rows)


def solution(mesh):
    return jax.shard_map(
        body,
        mesh=mesh,
        in_specs=(
            P(("dp", "tensor"), None),
            P(),
            P("dp", "tensor"),
            P("dp", "tensor"),
            P("dp", "tensor"),
            P("tensor", "dp"),
            P("dp"),
        ),
        out_specs=(P(("dp", "tensor"), None), P("dp", "tensor", None)),
        check_vma=False,
    )
```

profile of v0, /device:TPU:32, one launch (start us, length us, event | category | flops | bytes accessed | tf_op | source)
XLA Modules:
  0.0 671.7 jit_solution(11263055543441471757)
XLA Ops:
  7.2 0.0 all-gather.10.cloned.1.call-start
  7.2 0.7 all-gather.10.cloned.1.call-update
  7.9 0.0 all-gather.12.cloned.1.call-start
  7.9 0.7 all-gather.12.cloned.1.call-update
  8.6 0.0 all-gather.6.cloned.1.call-start
  8.7 0.7 convert_element_type.62
  9.4 1.1 fusion.11
  10.5 1.8 fusion.13
  12.3 0.0 all-gather.6.cloned.1.call-update
  12.3 0.0 all-gather.8.cloned.1.call-start
  12.4 0.5 all-gather.8.cloned.1.call-update
  12.9 0.0 all-gather.14.cloned.1.call-start
  13.0 0.5 all-gather.14.cloned.1.call-update
  13.5 0.0 reduce-scatter.2.cloned.1.call-start
  13.5 0.8 slice_compare_fusion
  14.4 0.1 fusion.30
  14.5 0.3 reduce-window.9
  14.8 0.1 slice.38
  14.9 0.1 slice_reduce_fusion
  15.0 0.7 broadcast_compare_fusion
  15.7 0.1 fusion.31
  15.8 0.9 fusion.23
  16.6 0.5 multiply_cosine_fusion
  17.2 118.4 %all-gather.10.cloned.1.call-done = bf16[4096,128]{1,0:T(8,128)(2,1)} async-done(((bf16[64,128]{1,0:T(8,128)(2,1)}), bf16[4096,128]{1,0:T(8,128)(2,1)}) %all-gather.10.cloned.1.call-update) | async-done | bytes 1048592 | tf_op jit(solution)/shard_map/all_gather | solution.py:68
  135.6 119.9 %all-gather.12.cloned.1.call-done = bf16[4096,128]{1,0:T(8,128)(2,1)} async-done(((bf16[64,128]{1,0:T(8,128)(2,1)}), bf16[4096,128]{1,0:T(8,128)(2,1)}) %all-gather.12.cloned.1.call-update) | async-done | bytes 1048592 | tf_op jit(solution)/shard_map/all_gather | solution.py:69
  255.5 69.0 %all-gather.6.cloned.1.call-done = bf16[256,4096]{1,0:T(8,128)(2,1)} async-done(((bf16[32,4096]{1,0:T(8,128)(2,1)}), bf16[256,4096]{1,0:T(8,128)(2,1)}) %all-gather.6.cloned.1.call-update) | async-done | bytes 2097168 | tf_op jit(solution)/shard_map/all_gather | solution.py:64
  324.5 123.7 %all-gather.8.cloned.1.call-done = bf16[4096,512]{1,0:T(8,128)(2,1)} async-done(((bf16[64,512]{1,0:T(8,128)(2,1)}), bf16[4096,512]{1,0:T(8,128)(2,1)}) %all-gather.8.cloned.1.call-update) | async-done | bytes 4194320 | tf_op jit(solution)/shard_map/all_gather | solution.py:67
  448.2 5.2 fusion
  453.4 0.1 slice.49
  453.5 0.2 reshape.129
  453.7 0.1 fusion.24
  453.8 0.2 fusion.26
  454.0 0.3 slice_negate_fusion
  454.4 0.4 maximum_multiply_fusion
  454.7 0.1 mul.123
  454.8 0.4 fusion.33
  455.2 0.2 fusion.9
  455.3 0.3 fusion.8
  455.7 114.6 %all-gather.14.cloned.1.call-done = bf16[512,4096]{0,1:T(8,128)(2,1)} async-done(((bf16[512,64]{0,1:T(8,128)(2,1)}), bf16[512,4096]{0,1:T(8,128)(2,1)}) %all-gather.14.cloned.1.call-update) | async-done | bytes 4194320 | tf_op jit(solution)/shard_map/all_gather | solution.py:107
  570.2 0.0 copy-start
  570.2 4.9 convolution_convert_fusion
  575.1 0.0 reduce-scatter.2.cloned.1.call-update
  575.1 0.7 pad_maximum_fusion.2
  575.8 87.3 %reduce-scatter.2.cloned.1.call-done = bf16[32,4096]{1,0:T(8,128)(2,1)} async-done(((bf16[256,4096]{1,0:T(8,128)(2,1)}), bf16[32,4096]{1,0:T(8,128)(2,1)}) %reduce-scatter.2.cloned.1.call-update) | async-done | bytes 262160 | tf_op jit(solution)/shard_map/reduce_scatter | solution.py:108
  663.1 0.0 copy-done
  663.1 1.7 fusion.14
  (5 shorter events, 0.1 us)
Async XLA Ops:
  7.2 128.5 %all-gather.10.cloned.1.call-start = ((), (), s32[]{:S(2)}) async-start(), calls=%async_computation.3 | async-start | bytes 1064960 | tf_op jit(solution)/shard_map/all_gather | solution.py:68
  7.9 247.6 %all-gather.12.cloned.1.call-start = ((), (), s32[]{:S(2)}) async-start(), calls=%async_computation.4 | async-start | bytes 1064960 | tf_op jit(solution)/shard_map/all_gather | solution.py:69
  8.6 315.9 %all-gather.6.cloned.1.call-start = ((), (), s32[]{:S(2)}) async-start(), calls=%async_computation.1 | async-start | bytes 2359296 | tf_op jit(solution)/shard_map/all_gather | solution.py:64
  12.3 435.9 %all-gather.8.cloned.1.call-start = ((), (), s32[]{:S(2)}) async-start(), calls=%async_computation.2 | async-start | bytes 4259840 | tf_op jit(solution)/shard_map/all_gather | solution.py:67
  12.9 557.3 %all-gather.14.cloned.1.call-start = ((), (), s32[]{:S(2)}) async-start(), calls=%async_computation.5 | async-start | bytes 4259840 | tf_op jit(solution)/shard_map/all_gather | solution.py:107
  13.5 649.6 %reduce-scatter.2.cloned.1.call-start = ((), (), s32[]{:S(2)}) async-start(), calls=%async_computation.6 | async-start | bytes 2359296 | tf_op jit(solution)/shard_map/reduce_scatter | solution.py:108
  570.2 92.9 %copy-start = (bf16[32,4096]{1,0:T(8,128)(2,1)S(1)}, bf16[32,4096]{1,0:T(8,128)(2,1)}, u32[]{:S(2)}) copy-start(bf16[32,4096]{1,0:T(8,128)(2,1)} %param.7) | copy-start | bytes 786436
Sparse Core Ops, SparseCore 0:
  10.1 125.4 all-gather.9
  137.8 117.6 all-gather.11
  259.3 65.1 all-gather.5
  326.5 121.6 all-gather.7
  450.2 119.9 all-gather.13
  575.2 87.8 reduce-scatter.1
where the time goes:
time: 672 us
  waiting for transfers between devices  635 us (94%)
  between operations  14.2 us (2%)
  matrix products  10.8 us (2%)
  other arithmetic  10.6 us (2%)
    all_gather x1, waiting for transfers between devices, body(): lax.all_gather(w_query, 'dp', axis=0, tiled=True)  124 us
    all_gather x1, waiting for transfers between devices, body(): lax.all_gather(w_value, 'dp', axis=0, tiled=True)  120 us
    all_gather x1, waiting for transfers between devices, body(): lax.all_gather(w_key, 'dp', axis=0, tiled=True)  118 us
    all_gather x1, waiting for transfers between devices, body(): out_full = lax.all_gather(w_out, 'dp', axis=1, tiled=True)  115 us
    reduce_scatter x1, waiting for transfers between devices, body(): lax.psum_scatter(jnp.dot(attended, out_full, preferred_element_type=jnp.f...  87.3 us
    all_gather x1, waiting for transfers between devices, body(): gathered = lax.all_gather(normed, 'tensor', axis=0, tiled=True)  69 us
  transfers between devices with their start and end apart: 6, of which 6 were waited for; matrix products, arithmetic and copies ran while one was open for 2% of the time, Pallas kernels for 0%

commit v1 on v0

--- a/solution.py
+++ b/solution.py
@@ -104,7 +104,9 @@
     attended = (
         jnp.transpose(mixed_rows, (2, 0, 1, 3)).astype(jnp.bfloat16).reshape(pack_rows, query_cols)
     )
-    out_full = lax.all_gather(w_out, "dp", axis=1, tiled=True)
+    out_full = jnp.concatenate(
+        lax.all_to_all(jnp.stack([w_out] * lax.axis_size("dp")), "dp", 0, 0), axis=1
+    )
     summed = lax.psum_scatter(
         jnp.dot(attended, out_full, preferred_element_type=jnp.float32).astype(jnp.bfloat16),
         "tensor",

time: 672 us -> 614 us (0.914)
  waiting for transfers between devices: 635 us -> 562 us
  starting transfers between devices: 0.23 us -> 17.2 us
    all_gather x1 -> x0, waiting for transfers between devices: 115 us -> none  [body(): out_full = lax.all_gather(w_out, 'dp', axis=1, tiled=True)]
    all_gather x1, waiting for transfers between devices: 118 us -> 156 us  [body(): lax.all_gather(w_key, 'dp', axis=0, tiled=True)]
    all_to_all x0 -> x1, starting transfers between devices: none -> 17 us  [body(): lax.all_to_all(jnp.stack([w_out] * lax.axis_size('dp')), 'dp', 0, 0)]
  transfers between devices with their start and end apart: 6 -> 6, of which waited for: 6 -> 5; matrix products, arithmetic and copies ran while one was open for 2% -> 2% of each run, Pallas kernels for 0% -> 0%
where the time goes in v1:
time: 614 us; the launch traced here: 613 us
  waiting for transfers between devices  562 us (92%)
  starting transfers between devices  17.2 us (3%)
  between operations  13.9 us (2%)
  matrix products  10.8 us (2%)
    all_gather x1, waiting for transfers between devices, body(): lax.all_gather(w_key, 'dp', axis=0, tiled=True)  156 us
    all_gather x1, waiting for transfers between devices, body(): lax.all_gather(w_query, 'dp', axis=0, tiled=True)  124 us
    all_gather x1, waiting for transfers between devices, body(): lax.all_gather(w_value, 'dp', axis=0, tiled=True)  123 us
    reduce_scatter x1, waiting for transfers between devices, body(): lax.psum_scatter(jnp.dot(attended, out_full, preferred_element_type=jnp.f...  87.3 us
    all_gather x1, waiting for transfers between devices, body(): gathered = lax.all_gather(normed, 'tensor', axis=0, tiled=True)  70 us
    all_to_all x1, starting transfers between devices, body(): lax.all_to_all(jnp.stack([w_out] * lax.axis_size('dp')), 'dp', 0, 0)  17 us
  transfers between devices with their start and end apart: 6, of which 5 were waited for; matrix products, arithmetic and copies ran while one was open for 2% of the time, Pallas kernels for 0%

profile of v1, /device:TPU:32, one launch (start us, length us, event | category | flops | bytes accessed | tf_op | source)
XLA Modules:
  0.0 613.4 jit_solution(9563754218986794006)
XLA Ops:
  7.2 0.0 all-gather.9.cloned.1.call-start
  7.2 0.7 all-gather.9.cloned.1.call-update
  7.9 0.0 all-gather.11.cloned.1.call-start
  7.9 0.7 all-gather.11.cloned.1.call-update
  8.6 3.3 stack.2
  12.0 0.0 copy-start.2
  12.0 0.0 copy-start
  12.0 0.0 copy-start.1
  12.0 17.0 %all-to-all-start = ((bf16[64,512,64]{1,2,0:T(8,128)(2,1)}), bf16[64,512,64]{1,2,0:T(8,128)(2,1)}, u32[]{:S(2)}, u32[]{:S(2)}) async-start(bf16[64,512,64]{1,2,0:T(8,128)(2,1)} %stack.2), calls=%async_computation | async-start | bytes 8388608 | tf_op jit(solution)/shard_map/all_to_all | solution.py:108
  29.0 0.0 all-gather.5.cloned.1.call-start
  29.0 0.0 copy-done.2
  29.0 0.0 copy-done
  29.1 0.2 fusion.11
  29.2 0.8 fusion.13
  30.1 0.0 all-gather.5.cloned.1.call-update
  30.1 0.0 all-gather.7.cloned.1.call-start
  30.2 0.5 all-gather.7.cloned.1.call-update
  30.7 0.0 reduce-scatter.2.cloned.1.call-start
  30.7 0.0 copy-done.1
  30.7 0.1 slice_compare_fusion
  30.8 0.1 fusion.30
  30.9 0.3 reduce-window.9
  31.2 0.1 slice.38
  31.3 0.1 slice_reduce_fusion
  31.5 0.1 fusion.31
  31.5 0.1 fusion.23
  31.7 0.5 multiply_cosine_fusion
  32.2 156.4 %all-gather.9.cloned.1.call-done = bf16[4096,128]{1,0:T(8,128)(2,1)} async-done(((bf16[64,128]{1,0:T(8,128)(2,1)}), bf16[4096,128]{1,0:T(8,128)(2,1)}) %all-gather.9.cloned.1.call-update) | async-done | bytes 1048592 | tf_op jit(solution)/shard_map/all_gather | solution.py:68
  188.6 122.5 %all-gather.11.cloned.1.call-done = bf16[4096,128]{1,0:T(8,128)(2,1)} async-done(((bf16[64,128]{1,0:T(8,128)(2,1)}), bf16[4096,128]{1,0:T(8,128)(2,1)}) %all-gather.11.cloned.1.call-update) | async-done | bytes 1048592 | tf_op jit(solution)/shard_map/all_gather | solution.py:69
  311.1 70.0 %all-gather.5.cloned.1.call-done = bf16[256,4096]{1,0:T(8,128)(2,1)} async-done(((bf16[32,4096]{1,0:T(8,128)(2,1)}), bf16[256,4096]{1,0:T(8,128)(2,1)}) %all-gather.5.cloned.1.call-update) | async-done | bytes 2097168 | tf_op jit(solution)/shard_map/all_gather | solution.py:64
  381.1 123.7 %all-gather.7.cloned.1.call-done = bf16[4096,512]{1,0:T(8,128)(2,1)} async-done(((bf16[64,512]{1,0:T(8,128)(2,1)}), bf16[4096,512]{1,0:T(8,128)(2,1)}) %all-gather.7.cloned.1.call-update) | async-done | bytes 4194320 | tf_op jit(solution)/shard_map/all_gather | solution.py:67
  504.8 5.2 fusion
  510.1 0.1 slice.49
  510.1 0.2 reshape.137
  510.4 0.1 fusion.24
  510.5 0.2 fusion.26
  510.6 0.3 slice_negate_fusion
  511.0 0.4 maximum_multiply_fusion
  511.3 0.1 mul.123
  511.4 0.4 fusion.33
  511.8 0.2 fusion.9
  512.0 0.3 fusion.8
  512.3 0.0 all-to-all-done
  512.3 4.8 convolution_convert_fusion
  517.1 0.0 reduce-scatter.2.cloned.1.call-update
  517.2 0.7 pad_maximum_fusion.2
  517.8 87.3 %reduce-scatter.2.cloned.1.call-done = bf16[32,4096]{1,0:T(8,128)(2,1)} async-done(((bf16[256,4096]{1,0:T(8,128)(2,1)}), bf16[32,4096]{1,0:T(8,128)(2,1)}) %reduce-scatter.2.cloned.1.call-update) | async-done | bytes 262160 | tf_op jit(solution)/shard_map/reduce_scatter | solution.py:110
  605.2 1.7 fusion.14
  (7 shorter events, 0.1 us)
Async XLA Ops:
  7.2 181.4 %all-gather.9.cloned.1.call-start = ((), (), s32[]{:S(2)}) async-start(), calls=%async_computation.4 | async-start | bytes 1064960 | tf_op jit(solution)/shard_map/all_gather | solution.py:68
  7.9 303.2 %all-gather.11.cloned.1.call-start = ((), (), s32[]{:S(2)}) async-start(), calls=%async_computation.5 | async-start | bytes 1064960 | tf_op jit(solution)/shard_map/all_gather | solution.py:69
  12.0 17.1 %copy-start.2 = (bf16[4096]{0:T(1024)(128)(2,1)S(1)}, bf16[4096]{0:T(1024)(128)(2,1)}, u32[]{:S(2)}) copy-start(bf16[4096]{0:T(1024)(128)(2,1)} %param.8) | copy-start | bytes 24580
  12.0 17.1 %copy-start = (bf16[32,4096]{1,0:T(8,128)(2,1)S(1)}, bf16[32,4096]{1,0:T(8,128)(2,1)}, u32[]{:S(2)}) copy-start(bf16[32,4096]{1,0:T(8,128)(2,1)} %param.7) | copy-start | bytes 786436
  12.0 18.8 %copy-start.1 = (s32[256]{0:T(256)S(1)}, s32[256]{0:T(256)}, u32[]{:S(2)}) copy-start(s32[256]{0:T(256)} %param.13) | copy-start | bytes 3076
  12.0 500.3 %all-to-all-start = ((bf16[64,512,64]{1,2,0:T(8,128)(2,1)}), bf16[64,512,64]{1,2,0:T(8,128)(2,1)}, u32[]{:S(2)}, u32[]{:S(2)}) async-start(bf16[64,512,64]{1,2,0:T(8,128)(2,1)} %stack.2), calls=%async_computation | async-start | bytes 8388608 | tf_op jit(solution)/shard_map/all_to_all | solution.py:108
  29.0 352.2 %all-gather.5.cloned.1.call-start = ((), (), s32[]{:S(2)}) async-start(), calls=%async_computation.2 | async-start | bytes 2359296 | tf_op jit(solution)/shard_map/all_gather | solution.py:64
  30.1 474.7 %all-gather.7.cloned.1.call-start = ((), (), s32[]{:S(2)}) async-start(), calls=%async_computation.3 | async-start | bytes 4259840 | tf_op jit(solution)/shard_map/all_gather | solution.py:67
  30.7 574.5 %reduce-scatter.2.cloned.1.call-start = ((), (), s32[]{:S(2)}) async-start(), calls=%async_computation.6 | async-start | bytes 2359296 | tf_op jit(solution)/shard_map/reduce_scatter | solution.py:110
Sparse Core Ops, SparseCore 0:
  10.1 178.4 all-gather.8
  190.7 120.3 all-gather.10
  314.9 66.1 all-gather.4
  383.1 121.6 all-gather.6
  517.3 87.8 reduce-scatter.1
